TPU v7x, 256 devices: a whole 4x4x8 slice. The times are simulated.
256 devices in a mesh: dp: 16 (over y_hi, z), seq: 16 (over x, y_lo, core).
Axes of the slice: x: 4, y: 4 (y_hi: 2, y_lo: 2; y = y_hi * 2 + y_lo), z: 8, core: 2. Of those that a mesh axis runs over, the one named last changes fastest.
Arguments:
- queries: bfloat16 [16, 2048, 2048], P('dp', 'seq'), may hold values from -6 to 6
- key_states: bfloat16 [16, 2048, 2048], P('dp', 'seq'), may hold values from -6 to 6
- value_states: bfloat16 [16, 2048, 2048], P('dp', 'seq'), may hold values from -6 to 6
- cotangent: bfloat16 [16, 2048, 2048], P('dp', 'seq'), may hold values from -6 to 6
- filter_taps: float32 [7, 2048], replicated, may hold values from -3 to 3
Outputs:
- conv_output: bfloat16 [16, 2048, 2048], P('dp', 'seq')
- grad_queries: bfloat16 [16, 2048, 2048], P('dp', 'seq')
- grad_keys: bfloat16 [16, 2048, 2048], P('dp', 'seq')
- grad_values: bfloat16 [16, 2048, 2048], P('dp', 'seq')
- filter_gradient: float32 [7, 2048], replicated
All inputs are finite; a program needn't handle non-finite values.
Results may differ from a plain program's by a relative error of at most 0.015.
Values may be sent and summed in bfloat16 or wider, within the bound.
No kernel may reach another device: no remote copies, remote signals or barrier semaphores. Data moves between devices by JAX's collectives and lax.ppermute only.
A program may use at most 128 MiB of HBM per device.

v0:
```python
import math
import jax
import jax.numpy as jnp
import numpy as np
from jax import lax
from jax.sharding import Mesh
from jax.sharding import PartitionSpec as P

HD = 128
TAPS = 7
GROUP_HEADS = 2
SEQ = ("sc", "core")


def padded(value, width):
    peers = lax.axis_size("sc") * lax.axis_size("core")
    length = value.shape[0]
    up = [(i, (i + 1) % peers) for i in range(peers)]
    down = [(j, i) for i, j in up]
    before = lax.ppermute(value[length - width :], SEQ, up)
    after = lax.ppermute(value[:width], SEQ, down)
    return jnp.concatenate([before, value, after], axis=0)


def to_chip_rows(value):
    rows, channels = value.shape
    split = value.reshape(rows, 2, channels // 2)
    return lax.all_to_all(split, "core", 1, 0, tiled=True).reshape(2 * rows, channels // 2)


def from_chip_rows(value):
    rows2, half = value.shape
    split = value.reshape(2, rows2 // 2, 1, half)
    out = lax.all_to_all(split, "core", 0, 2, tiled=True)
    return out.reshape(rows2 // 2, 2 * half)


def on_device(queries, key_states, value_states, cotangent, filter_taps):
    tok_rows = queries.shape[1]
    channels = queries.shape[2]
    chips = lax.axis_size("sc")
    seq_total = tok_rows * chips * 2
    chip_rows = 2 * tok_rows
    half_channels = channels // 2
    head_count = half_channels // HD
    group_width = GROUP_HEADS * HD
    group_count = head_count // GROUP_HEADS
    score_scale = HD ** (-0.5)
    half_width = (TAPS - 1) // 2
    local_q = queries[0]
    local_k = key_states[0]
    local_v = value_states[0]
    local_g = cotangent[0]
    grad_pad = padded(local_g, half_width)
    grad_sum = jnp.zeros((tok_rows, channels), jnp.float32)
    for tap_index in range(TAPS):
        start_row = 2 * half_width - tap_index
        grad_sum = grad_sum + filter_taps[tap_index] * grad_pad[
            start_row : start_row + tok_rows
        ].astype(jnp.float32)
    grad_attn = grad_sum.astype(jnp.bfloat16)
    chip_q = to_chip_rows(local_q)
    chip_k = to_chip_rows(local_k)
    chip_v = to_chip_rows(local_v)
    chip_d = to_chip_rows(grad_attn)
    chip_index = lax.axis_index("sc")
    query_pos = chip_index * chip_rows + jnp.arange(chip_rows, dtype=jnp.int32)
    key_pos = jnp.arange(seq_total, dtype=jnp.int32)
    visible = query_pos[:, None] >= key_pos[None, :]
    attended_parts, grad_q_parts, key_parts, value_parts = ([], [], [], [])
    for group_index in range(group_count):
        cols = slice(group_index * group_width, (group_index + 1) * group_width)
        k_all = lax.all_gather(chip_k[:, cols], "sc", axis=0, tiled=True)
        v_all = lax.all_gather(chip_v[:, cols], "sc", axis=0, tiled=True)
        q_part = chip_q[:, cols].reshape(chip_rows, GROUP_HEADS, HD)
        d_part = chip_d[:, cols].reshape(chip_rows, GROUP_HEADS, HD)
        k_part = k_all.reshape(seq_total, GROUP_HEADS, HD)
        v_part = v_all.reshape(seq_total, GROUP_HEADS, HD)
        scores = (
            jnp.einsum("thd,uhd->htu", q_part, k_part, preferred_element_type=jnp.float32)
            * score_scale
        )
        row_top = jnp.max(jnp.where(visible, scores, -jnp.inf), -1, keepdims=True)
        raw = jnp.where(visible, jnp.exp(scores - row_top), 0.0)
        row_total = jnp.sum(raw, -1, keepdims=True)
        probs = raw / row_total
        probs_low = probs.astype(jnp.bfloat16)
        attended = jnp.einsum("htu,uhd->thd", probs_low, v_part, preferred_element_type=jnp.float32)
        attended_parts.append(attended.astype(jnp.bfloat16).reshape(chip_rows, group_width))
        dprob = jnp.einsum("thd,uhd->htu", d_part, v_part, preferred_element_type=jnp.float32)
        row_delta = jnp.sum(probs * dprob, -1, keepdims=True)
        dscore = (probs * (dprob - row_delta) * score_scale).astype(jnp.bfloat16)
        grad_q = jnp.einsum("htu,uhd->thd", dscore, k_part, preferred_element_type=jnp.float32)
        grad_q_parts.append(grad_q.astype(jnp.bfloat16).reshape(chip_rows, group_width))
        key_term = jnp.einsum("htu,thd->uhd", dscore, q_part, preferred_element_type=jnp.float32)
        value_term = jnp.einsum(
            "htu,thd->uhd", probs_low, d_part, preferred_element_type=jnp.float32
        )
        key_parts.append(
            lax.psum_scatter(
                key_term.astype(jnp.bfloat16).reshape(seq_total, group_width),
                "sc",
                scatter_dimension=0,
                tiled=True,
            )
        )
        value_parts.append(
            lax.psum_scatter(
                value_term.astype(jnp.bfloat16).reshape(seq_total, group_width),
                "sc",
                scatter_dimension=0,
                tiled=True,
            )
        )
    attn_out = from_chip_rows(jnp.concatenate(attended_parts, axis=1))
    grad_queries = from_chip_rows(jnp.concatenate(grad_q_parts, axis=1))
    grad_keys = from_chip_rows(jnp.concatenate(key_parts, axis=1))
    grad_values = from_chip_rows(jnp.concatenate(value_parts, axis=1))
    out_pad = padded(attn_out, half_width)
    conv_sum = jnp.zeros((tok_rows, channels), jnp.float32)
    filter_rows = []
    local_gf = local_g.astype(jnp.float32)
    for tap_index in range(TAPS):
        moved = out_pad[tap_index : tap_index + tok_rows].astype(jnp.float32)
        conv_sum = conv_sum + filter_taps[tap_index] * moved
        filter_rows.append(jnp.sum(moved * local_gf, 0))
    filter_gradient = lax.psum(jnp.stack(filter_rows, 0), ("dp", "sc", "core"))
    conv_output = conv_sum.astype(jnp.bfloat16)
    return (
        conv_output[None],
        grad_queries[None],
        grad_keys[None],
        grad_values[None],
        filter_gradient,
    )


def solution(mesh):
    devices = np.asarray(mesh.devices)
    dp_size, seq_size = devices.shape
    split_mesh = Mesh(devices.reshape(dp_size, seq_size // 2, 2), ("dp", "sc", "core"))
    block = P("dp", SEQ, None)
    in_specs = (block, block, block, block, P())
    out_specs = (block, block, block, block, P())
    return jax.shard_map(
        on_device, mesh=split_mesh, in_specs=in_specs, out_specs=out_specs, check_vma=False
    )
```

profile of v0, /device:TPU:1, one launch (start us, length us, event | category | flops | bytes accessed | tf_op | source)
XLA Modules:
  0.0 740.7 jit_solution(332086236696625652)
XLA Ops:
  8.6 7.2 all_to_all.120
  17.2 4.2 all_to_all.121
  36.2 20.8 %collective-permute-done.2 = bf16[3,2048]{0,1:T(8,128)(2,1)S(1)} collective-permute-done((bf16[3,2048]{0,1:T(8,128)(2,1)}, bf16[3,2048]{0,1:T(8,128)(2,1)S(1)}, u32[]{:S(2)}, u32[]{:S(2)}) %collective-permute-start.2) | collective-permute-done | bytes 12320 | tf_op jit(solution)/shard_map/ppermute | solution.py:21
  58.1 5.9 fusion.115
  71.0 34.5 %all-gather.15.cloned.1.call-done = bf16[2048,256]{1,0:T(8,128)(2,1)} async-done(((bf16[256,256]{1,0:T(8,128)(2,1)}), bf16[2048,256]{1,0:T(8,128)(2,1)}) %all-gather.15.cloned.1.call-update) | async-done | bytes 1048592 | tf_op jit(solution)/shard_map/all_gather | solution.py:74
  110.6 5.9 fusion.180
  116.5 9.7 %convolution_convert_fusion.2 = bf16[2,2048,128]{1,2,0:T(8,128)(2,1)} fusion(bf16[256,2,128]{0,2,1:T(8,128)(2,1)} %bitcast.232, f32[2,256,2048]{2,1,0:T(8,128)} %fusion.183, f32[2,256,2048]{2,1,0:T(8,128)} %get-tuple-element.66, f32[2,256]{1,0:T(2,128)} %get-tuple-element.65), kind=kOutput, calls=%fused_computation.45 | convolution fusion | flops 276302336 | bytes 9570304 | tf_op jit(solution)/shard_map/htu,thd->uhd/dot_general | solution.py:95
  127.9 19.7 %all-gather.17.cloned.1.call-done = bf16[2048,256]{1,0:T(8,128)(2,1)} async-done(((bf16[256,256]{1,0:T(8,128)(2,1)}), bf16[2048,256]{1,0:T(8,128)(2,1)}) %all-gather.17.cloned.1.call-update) | async-done | bytes 1048592 | tf_op jit(solution)/shard_map/all_gather | solution.py:73
  149.9 41.5 %all-gather.19.cloned.1.call-done = bf16[2048,256]{1,0:T(8,128)(2,1)} async-done(((bf16[256,256]{1,0:T(8,128)(2,1)}), bf16[2048,256]{1,0:T(8,128)(2,1)}) %all-gather.19.cloned.1.call-update) | async-done | bytes 1048592 | tf_op jit(solution)/shard_map/all_gather | solution.py:74
  196.5 6.5 fusion.179
  203.1 9.7 %convolution_convert_fusion.1 = bf16[2,2048,128]{1,2,0:T(8,128)(2,1)} fusion(bf16[256,2,128]{0,2,1:T(8,128)(2,1)} %bitcast.236, f32[2,256,2048]{2,1,0:T(8,128)} %fusion.184, f32[2,256,2048]{2,1,0:T(8,128)} %get-tuple-element.64, f32[2,256]{1,0:T(2,128)} %get-tuple-element.63), kind=kOutput, calls=%fused_computation.44 | convolution fusion | flops 276302336 | bytes 9570304 | tf_op jit(solution)/shard_map/htu,thd->uhd/dot_general | solution.py:95
  214.6 19.3 %all-gather.21.cloned.1.call-done = bf16[2048,256]{1,0:T(8,128)(2,1)} async-done(((bf16[256,256]{1,0:T(8,128)(2,1)}), bf16[2048,256]{1,0:T(8,128)(2,1)}) %all-gather.21.cloned.1.call-update) | async-done | bytes 1048592 | tf_op jit(solution)/shard_map/all_gather | solution.py:73
  236.1 41.4 %all-gather.23.cloned.1.call-done = bf16[2048,256]{1,0:T(8,128)(2,1)} async-done(((bf16[256,256]{1,0:T(8,128)(2,1)}), bf16[2048,256]{1,0:T(8,128)(2,1)}) %all-gather.23.cloned.1.call-update) | async-done | bytes 1048592 | tf_op jit(solution)/shard_map/all_gather | solution.py:74
  283.7 6.5 fusion.178
  290.2 9.7 %convolution_convert_fusion = bf16[2,2048,128]{1,2,0:T(8,128)(2,1)} fusion(bf16[256,2,128]{0,2,1:T(8,128)(2,1)} %bitcast.238, f32[2,256,2048]{2,1,0:T(8,128)} %fusion.185, f32[2,256,2048]{2,1,0:T(8,128)} %get-tuple-element.62, f32[2,256]{1,0:T(2,128)} %get-tuple-element.61), kind=kOutput, calls=%fused_computation.43 | convolution fusion | flops 276302336 | bytes 9570304 | tf_op jit(solution)/shard_map/htu,thd->uhd/dot_general | solution.py:95
  301.1 18.5 %all-gather.9.cloned.1.call-done = bf16[2048,256]{1,0:T(8,128)(2,1)} async-done(((bf16[256,256]{1,0:T(8,128)(2,1)}), bf16[2048,256]{1,0:T(8,128)(2,1)}) %all-gather.9.cloned.1.call-update) | async-done | bytes 1048592 | tf_op jit(solution)/shard_map/all_gather | solution.py:73
  321.9 42.0 %all-gather.11.cloned.1.call-done = bf16[2048,256]{1,0:T(8,128)(2,1)} async-done(((bf16[256,256]{1,0:T(8,128)(2,1)}), bf16[2048,256]{1,0:T(8,128)(2,1)}) %all-gather.11.cloned.1.call-update) | async-done | bytes 1048592 | tf_op jit(solution)/shard_map/all_gather | solution.py:74
  370.0 6.0 fusion.181
  376.0 9.6 %convolution_convert_fusion.3 = bf16[2,2048,128]{1,2,0:T(8,128)(2,1)} fusion(bf16[256,2,128]{0,2,1:T(8,128)(2,1)S(1)} %bitcast.234, f32[2,256,2048]{2,1,0:T(8,128)} %fusion.182, f32[2,256,2048]{2,1,0:T(8,128)} %get-tuple-element.68, f32[2,256]{1,0:T(2,128)S(1)} %get-tuple-element.67), kind=kOutput, calls=%fused_computation.46 | convolution fusion | flops 276302336 | bytes 9570304 | tf_op jit(solution)/shard_map/htu,thd->uhd/dot_general | solution.py:95
  396.6 8.2 %fusion.91 = bf16[256,2,128]{2,0,1:T(8,128)(2,1)S(1)} fusion(bf16[2048,2,128]{0,2,1:T(8,128)(2,1)} %bitcast.215, f32[2,256,2048]{2,1,0:T(8,128)} %fusion.183, f32[2,256,2048]{2,1,0:T(8,128)} %get-tuple-element.66, f32[2,256]{1,0:T(2,128)S(1)} %copy-done.23), kind=kOutput, calls=%fused_computation.111 | convolution fusion | flops 275843584 | bytes 9570304 | tf_op jit(solution)/shard_map/htu,uhd->thd/dot_general | solution.py:93
  412.7 7.9 %fusion.94 = bf16[256,2,128]{2,0,1:T(8,128)(2,1)S(1)} fusion(bf16[2048,2,128]{0,2,1:T(8,128)(2,1)S(1)} %bitcast.217, f32[2,256,2048]{2,1,0:T(8,128)} %fusion.184, f32[2,256,2048]{2,1,0:T(8,128)} %get-tuple-element.64, f32[2,256]{1,0:T(2,128)S(1)} %copy-done.24), kind=kOutput, calls=%fused_computation.112 | convolution fusion | flops 275843584 | bytes 9570304 | tf_op jit(solution)/shard_map/htu,uhd->thd/dot_general | solution.py:93
  429.3 8.1 %fusion.97 = bf16[256,2,128]{2,0,1:T(8,128)(2,1)S(1)} fusion(bf16[2048,2,128]{0,2,1:T(8,128)(2,1)S(1)} %bitcast.219, f32[2,256,2048]{2,1,0:T(8,128)} %fusion.185, f32[2,256,2048]{2,1,0:T(8,128)} %get-tuple-element.62, f32[2,256]{1,0:T(2,128)} %get-tuple-element.61), kind=kOutput, calls=%fused_computation.113 | convolution fusion | flops 275843584 | bytes 9570304 | tf_op jit(solution)/shard_map/htu,uhd->thd/dot_general | solution.py:93
  437.9 8.0 %fusion.88 = bf16[256,2,128]{2,0,1:T(8,128)(2,1)S(1)} fusion(bf16[2048,2,128]{0,2,1:T(8,128)(2,1)S(1)} %bitcast.221, f32[2,256,2048]{2,1,0:T(8,128)} %fusion.182, f32[2,256,2048]{2,1,0:T(8,128)} %get-tuple-element.68, f32[2,256]{1,0:T(2,128)} %copy-done.26), kind=kOutput, calls=%fused_computation.110 | convolution fusion | flops 275843584 | bytes 9570304 | tf_op jit(solution)/shard_map/htu,uhd->thd/dot_general | solution.py:93
  447.1 8.7 %all-to-all-start.3 = ((bf16[2,128,1,1024]{3,1,2,0:T(8,128)(2,1)}), bf16[2,128,1,1024]{3,1,2,0:T(8,128)(2,1)S(1)}, u32[]{:S(2)}, u32[]{:S(2)}) async-start(bf16[2,128,1,1024]{3,1,2,0:T(8,128)(2,1)} %maximum_bitcast_fusion), calls=%async_computation.3 | async-start | bytes 1048576 | tf_op jit(solution)/shard_map/all_to_all | solution.py:34
  464.4 7.4 collective-permute-done.1
  480.0 81.5 %psum.7 = f32[7,2048]{1,0:T(8,128)} all-reduce(f32[7,2048]{1,0:T(8,128)S(1)} %stack.31), channel_id=1, replica_groups=mesh['dp'=16,'sc'=8,'core'=2] {'dp','sc','core'}, use_global_device_ids=true, to_apply=%region_27.28 | all-reduce | flops 14336 | bytes 114688 | tf_op jit(solution)/shard_map/psum | solution.py:127
  563.0 23.9 %reduce-scatter.19.cloned.1.call-done = bf16[256,256]{0,1:T(8,128)(2,1)} async-done(((bf16[2048,256]{0,1:T(8,128)(2,1)}), bf16[256,256]{0,1:T(8,128)(2,1)}) %reduce-scatter.19.cloned.1.call-update) | async-done | bytes 131088 | tf_op jit(solution)/shard_map/reduce_scatter | solution.py:108
  586.8 43.3 %reduce-scatter.21.cloned.1.call-done = bf16[256,256]{0,1:T(8,128)(2,1)} async-done(((bf16[2048,256]{0,1:T(8,128)(2,1)}), bf16[256,256]{0,1:T(8,128)(2,1)}) %reduce-scatter.21.cloned.1.call-update) | async-done | bytes 131088 | tf_op jit(solution)/shard_map/reduce_scatter | solution.py:108
  630.1 43.4 %reduce-scatter.23.cloned.1.call-done = bf16[256,256]{0,1:T(8,128)(2,1)} async-done(((bf16[2048,256]{0,1:T(8,128)(2,1)}), bf16[256,256]{0,1:T(8,128)(2,1)}) %reduce-scatter.23.cloned.1.call-update) | async-done | bytes 131088 | tf_op jit(solution)/shard_map/reduce_scatter | solution.py:108
  673.5 43.4 %reduce-scatter.17.cloned.1.call-done = bf16[256,256]{0,1:T(8,128)(2,1)} async-done(((bf16[2048,256]{0,1:T(8,128)(2,1)}), bf16[256,256]{0,1:T(8,128)(2,1)}) %reduce-scatter.17.cloned.1.call-update) | async-done | bytes 131088 | tf_op jit(solution)/shard_map/reduce_scatter | solution.py:108
  718.3 9.0 %all_to_all.123 = bf16[2,128,1,1024]{3,1,2,0:T(8,128)(2,1)S(1)} all-to-all(bf16[2,128,1,1024]{3,1,2,0:T(8,128)(2,1)S(1)} %bitcast.199), channel_id=1, replica_groups=mesh['dp'=16,'sc'=8,'core'=2] {'core'}, dimensions={0} | all-to-all | bytes 1048576 | tf_op jit(solution)/shard_map/all_to_all | solution.py:34
  728.5 4.1 all_to_all.124
  (187 shorter events, 110.5 us)
Async XLA Ops:
  7.2 62.3 %all-gather.13.cloned.1.call-start = ((), (), s32[]{:S(2)}) async-start(), calls=%async_computation.18 | async-start | bytes 1179648 | tf_op jit(solution)/shard_map/all_gather | solution.py:73
  8.6 17.0 %copy-start.7 = (bf16[1,128,2048]{2,1,0:T(8,128)(2,1)S(1)}, bf16[1,128,2048]{2,1,0:T(8,128)(2,1)}, u32[]{:S(2)}) copy-start(bf16[1,128,2048]{2,1,0:T(8,128)(2,1)} %param.5) | copy-start | bytes 1572868
  16.8 88.7 %all-gather.15.cloned.1.call-start = ((), (), s32[]{:S(2)}) async-start(), calls=%async_computation.19 | async-start | bytes 1179648 | tf_op jit(solution)/shard_map/all_gather | solution.py:74
  22.4 125.3 %all-gather.17.cloned.1.call-start = ((), (), s32[]{:S(2)}) async-start(), calls=%async_computation.20 | async-start | bytes 1179648 | tf_op jit(solution)/shard_map/all_gather | solution.py:73
  23.1 168.3 %all-gather.19.cloned.1.call-start = ((), (), s32[]{:S(2)}) async-start(), calls=%async_computation.21 | async-start | bytes 1179648 | tf_op jit(solution)/shard_map/all_gather | solution.py:74
  23.7 210.2 %all-gather.21.cloned.1.call-start = ((), (), s32[]{:S(2)}) async-start(), calls=%async_computation.22 | async-start | bytes 1179648 | tf_op jit(solution)/shard_map/all_gather | solution.py:73
  24.3 253.2 %all-gather.23.cloned.1.call-start = ((), (), s32[]{:S(2)}) async-start(), calls=%async_computation.23 | async-start | bytes 1179648 | tf_op jit(solution)/shard_map/all_gather | solution.py:74
  24.8 294.7 %all-gather.9.cloned.1.call-start = ((), (), s32[]{:S(2)}) async-start(), calls=%async_computation.16 | async-start | bytes 1179648 | tf_op jit(solution)/shard_map/all_gather | solution.py:73
  26.6 8.0 %all-to-all-start = ((bf16[128,2,1024]{0,2,1:T(8,128)(2,1)}), bf16[128,2,1024]{0,2,1:T(8,128)(2,1)S(1)}, u32[]{:S(2)}, u32[]{:S(2)}) async-start(bf16[128,2,1024]{0,2,1:T(8,128)(2,1)} %bitcast.1), calls=%async_computation | async-start | bytes 1048576 | tf_op jit(solution)/shard_map/all_to_all | solution.py:28
  30.5 333.4 %all-gather.11.cloned.1.call-start = ((), (), s32[]{:S(2)}) async-start(), calls=%async_computation.17 | async-start | bytes 1179648 | tf_op jit(solution)/shard_map/all_gather | solution.py:74
  31.7 25.3 %collective-permute-start.2 = (bf16[3,2048]{0,1:T(8,128)(2,1)}, bf16[3,2048]{0,1:T(8,128)(2,1)S(1)}, u32[]{:S(2)}, u32[]{:S(2)}) collective-permute-start(bf16[3,2048]{0,1:T(8,128)(2,1)} %get-tuple-element.38), channel_id=1, source_target_pairs={{1,0},{2,1},{3,2},{4,3},{5,4},{6,5},{7,6},{8,7},{9,8},{10,9},{11,1... | collective-permute-start | bytes 36872 | tf_op jit(solution)/shard_map/ppermute | solution.py:21
  31.8 26.3 %collective-permute-start.3 = (bf16[3,2048]{0,1:T(8,128)(2,1)S(1)}, bf16[3,2048]{0,1:T(8,128)(2,1)}, u32[]{:S(2)}, u32[]{:S(2)}) collective-permute-start(bf16[3,2048]{0,1:T(8,128)(2,1)S(1)} %get-tuple-element.39), channel_id=1, source_target_pairs={{0,1},{1,2},{2,3},{3,4},{4,5},{5,6},{6,7},{7,8},{8,9},{9,10},{10,1... | collective-permute-start | bytes 36872 | tf_op jit(solution)/shard_map/ppermute | solution.py:20
  33.5 528.1 %reduce-scatter.11.cloned.1.call-start = ((), (), s32[]{:S(2)}) async-start(), calls=%async_computation.25 | async-start | bytes 1179648 | tf_op jit(solution)/shard_map/reduce_scatter | solution.py:100
  71.0 45.5 %copy-start.2 = (bf16[2048,256]{0,1:T(8,128)(2,1)}, bf16[2048,256]{0,1:T(8,128)(2,1)S(1)}, u32[]{:S(2)}) copy-start(bf16[2048,256]{0,1:T(8,128)(2,1)S(1)} %copy.289) | copy-start | bytes 3145732
  126.1 435.4 %reduce-scatter.13.cloned.1.call-start = ((), (), s32[]{:S(2)}) async-start(), calls=%async_computation.26 | async-start | bytes 1179648 | tf_op jit(solution)/shard_map/reduce_scatter | solution.py:100
  212.8 348.8 %reduce-scatter.15.cloned.1.call-start = ((), (), s32[]{:S(2)}) async-start(), calls=%async_computation.27 | async-start | bytes 1179648 | tf_op jit(solution)/shard_map/reduce_scatter | solution.py:100
  300.0 261.6 %reduce-scatter.9.cloned.1.call-start = ((), (), s32[]{:S(2)}) async-start(), calls=%async_computation.24 | async-start | bytes 1179648 | tf_op jit(solution)/shard_map/reduce_scatter | solution.py:100
  301.1 68.9 %copy-start.13 = (bf16[256,256]{0,1:T(8,128)(2,1)}, bf16[256,256]{0,1:T(8,128)(2,1)S(1)}, u32[]{:S(2)}) copy-start(bf16[256,256]{0,1:T(8,128)(2,1)S(1)} %copy.319) | copy-start | bytes 393220
  321.9 48.2 %copy-start.15 = (bf16[256,256]{0,1:T(8,128)(2,1)S(1)}, bf16[256,256]{0,1:T(8,128)(2,1)}, u32[]{:S(2)}) copy-start(bf16[256,256]{0,1:T(8,128)(2,1)} %copy.277) | copy-start | bytes 393220
  385.7 201.1 %reduce-scatter.19.cloned.1.call-start = ((), (), s32[]{:S(2)}) async-start(), calls=%async_computation.29 | async-start | bytes 1179648 | tf_op jit(solution)/shard_map/reduce_scatter | solution.py:108
  389.5 240.6 %reduce-scatter.21.cloned.1.call-start = ((), (), s32[]{:S(2)}) async-start(), calls=%async_computation.30 | async-start | bytes 1179648 | tf_op jit(solution)/shard_map/reduce_scatter | solution.py:108
  393.4 280.1 %reduce-scatter.23.cloned.1.call-start = ((), (), s32[]{:S(2)}) async-start(), calls=%async_computation.31 | async-start | bytes 1179648 | tf_op jit(solution)/shard_map/reduce_scatter | solution.py:108
  412.2 304.7 %reduce-scatter.17.cloned.1.call-start = ((), (), s32[]{:S(2)}) async-start(), calls=%async_computation.28 | async-start | bytes 1179648 | tf_op jit(solution)/shard_map/reduce_scatter | solution.py:108
  447.1 10.0 %all-to-all-start.3 = ((bf16[2,128,1,1024]{3,1,2,0:T(8,128)(2,1)}), bf16[2,128,1,1024]{3,1,2,0:T(8,128)(2,1)S(1)}, u32[]{:S(2)}, u32[]{:S(2)}) async-start(bf16[2,128,1,1024]{3,1,2,0:T(8,128)(2,1)} %maximum_bitcast_fusion), calls=%async_computation.3 | async-start | bytes 1048576 | tf_op jit(solution)/shard_map/all_to_all | solution.py:34
  456.6 15.2 %copy-start.16 = (f32[1,2048]{1,0:T(1,128)S(1)}, f32[1,2048]{1,0:T(1,128)}, u32[]{:S(2)}) copy-start(f32[1,2048]{1,0:T(1,128)} %get-tuple-element.56) | copy-start | bytes 24580
  456.6 15.2 %copy-start.17 = (f32[1,2048]{1,0:T(1,128)S(1)}, f32[1,2048]{1,0:T(1,128)}, u32[]{:S(2)}) copy-start(f32[1,2048]{1,0:T(1,128)} %get-tuple-element.57) | copy-start | bytes 24580
  456.6 15.2 %copy-start.18 = (f32[1,2048]{1,0:T(1,128)S(1)}, f32[1,2048]{1,0:T(1,128)}, u32[]{:S(2)}) copy-start(f32[1,2048]{1,0:T(1,128)} %get-tuple-element.58) | copy-start | bytes 24580
  456.6 15.2 %copy-start.19 = (f32[1,2048]{1,0:T(1,128)S(1)}, f32[1,2048]{1,0:T(1,128)}, u32[]{:S(2)}) copy-start(f32[1,2048]{1,0:T(1,128)} %get-tuple-element.59) | copy-start | bytes 24580
  456.6 15.2 %copy-start.20 = (f32[1,2048]{1,0:T(1,128)S(1)}, f32[1,2048]{1,0:T(1,128)}, u32[]{:S(2)}) copy-start(f32[1,2048]{1,0:T(1,128)} %get-tuple-element.60) | copy-start | bytes 24580
  457.1 5.6 all-to-all-start.5
  461.7 2.4 collective-permute-start
  461.7 10.0 %collective-permute-start.1 = (bf16[3,2048]{0,1:T(8,128)(2,1)S(1)}, bf16[3,2048]{0,1:T(8,128)(2,1)S(1)}, u32[]{:S(2)}, u32[]{:S(2)}) collective-permute-start(bf16[3,2048]{0,1:T(8,128)(2,1)S(1)} %bitcast.222), channel_id=1, source_target_pairs={{1,0},{2,1},{3,2},{4,3},{5,4},{6,5},{7,6},{8,7},{9,8},{10,9},{11,1... | collective-permute-start | bytes 36872 | tf_op jit(solution)/shard_map/ppermute | solution.py:21
  (19 other events, 134.5 us)
Sparse Core Ops, SparseCore 0:
  16.9 45.7 all-gather.12
  64.6 40.9 all-gather.14
  107.3 40.2 all-gather.16
  149.3 42.1 all-gather.18
  193.0 40.7 all-gather.20
  236.1 41.3 all-gather.22
  279.3 40.2 all-gather.8
  321.9 41.8 all-gather.10
  366.4 41.0 reduce-scatter.10
  409.8 41.1 reduce-scatter.12
  453.5 44.8 reduce-scatter.14
  500.8 42.3 reduce-scatter.8
  545.8 41.0 reduce-scatter.18
  589.2 40.8 reduce-scatter.20
  632.5 40.9 reduce-scatter.22
  675.9 40.9 reduce-scatter.16
where the time goes:
time: 750 us; the launch traced here: 741 us
  waiting for transfers between devices  404 us (54%)
  matrix products  136 us (18%)
  blocking collectives  110 us (15%)
  local copies, waits for them, and re-layouts  38.6 us (5%)
  starting transfers between devices  20.2 us (3%)
  other arithmetic  17.8 us (2%)
  between operations  14.8 us (2%)
    all_gather x4, waiting for transfers between devices, on_device(): v_all = lax.all_gather(chip_v[:, cols], 'sc', axis=0, tiled=True)  159 us
    reduce_scatter x4, waiting for transfers between devices, on_device(): lax.psum_scatter(value_term.astype(jnp.bfloat16).reshape(seq_total, group...  154 us
    psum x1, blocking collectives, on_device(): filter_gradient = lax.psum(jnp.stack(filter_rows, 0), ('dp', 'sc', 'core'))  81.5 us
    all_gather x4, waiting for transfers between devices, on_device(): k_all = lax.all_gather(chip_k[:, cols], 'sc', axis=0, tiled=True)  57.5 us
    dot_general x4, matrix products, on_device(): jnp.einsum('htu,thd->uhd', dscore, q_part, preferred_element_type=jnp.flo...  38.7 us
    dot_general x4, matrix products, on_device(): jnp.einsum('htu,uhd->thd', dscore, k_part, preferred_element_type=jnp.flo...  32.2 us
    ppermute x2, waiting for transfers between devices, padded(): after = lax.ppermute(value[:width], SEQ, down)  28.2 us
    sub x4, matrix products, on_device(): raw = jnp.where(visible, jnp.exp(scores - row_top), 0.0)  24.9 us
  transfers between devices with their start and end apart: 23, of which 15 were waited for; matrix products, arithmetic and copies ran while one was open for 25% of the time, Pallas kernels for 0%

commit v1 on v0

--- a/solution.py
+++ b/solution.py
@@ -124,7 +124,9 @@
         moved = out_pad[tap_index : tap_index + tok_rows].astype(jnp.float32)
         conv_sum = conv_sum + filter_taps[tap_index] * moved
         filter_rows.append(jnp.sum(moved * local_gf, 0))
-    filter_gradient = lax.psum(jnp.stack(filter_rows, 0), ("dp", "sc", "core"))
+    filter_gradient = jnp.sum(
+        lax.all_gather(jnp.stack(filter_rows, 0), ("dp", "sc", "core")), axis=0
+    )
     conv_output = conv_sum.astype(jnp.bfloat16)
     return (
         conv_output[None],

time: 750 us -> 1180 us (1.57)
  waiting for transfers between devices: 404 us -> 902 us
  blocking collectives: 110 us -> 41.5 us
  starting transfers between devices: 20.2 us -> 7.6 us
    all_gather x0 -> x1, waiting for transfers between devices: none -> 418 us  [on_device(): lax.all_gather(jnp.stack(filter_rows, 0), ('dp', 'sc', 'core'))]
    psum x1 -> x0, blocking collectives: 81.5 us -> none  [on_device(): filter_gradient = lax.psum(jnp.stack(filter_rows, 0), ('dp', 'sc', 'core'))]
    reduce_scatter x4, waiting for transfers between devices: 0.03 us -> 57.8 us  [on_device(): lax.psum_scatter(key_term.astype(jnp.bfloat16).reshape(seq_total, group_w...]
    reduce_scatter x4, waiting for transfers between devices: 154 us -> 173 us  [on_device(): lax.psum_scatter(value_term.astype(jnp.bfloat16).reshape(seq_total, group...]
    all_to_all x2 -> x4, blocking collectives: 13.1 us -> 26.4 us  [from_chip_rows(): out = lax.all_to_all(split, 'core', 0, 2, tiled=True)]
    all_to_all x2 -> x0, starting transfers between devices: 12.5 us -> none  [from_chip_rows(): out = lax.all_to_all(split, 'core', 0, 2, tiled=True)]
  transfers between devices with their start and end apart: 23 -> 22, of which waited for: 15 -> 18; matrix products, arithmetic and copies ran while one was open for 25% -> 16% of each run, Pallas kernels for 0% -> 0%
where the time goes in v1:
time: 1180 us; the launch traced here: 1170 us
  waiting for transfers between devices  902 us (76%)
  matrix products  139 us (12%)
  blocking collectives  41.5 us (4%)
  local copies, waits for them, and re-layouts  38.7 us (3%)
  other arithmetic  23.7 us (2%)
  between operations  14.8 us (1%)
    all_gather x1, waiting for transfers between devices, on_device(): lax.all_gather(jnp.stack(filter_rows, 0), ('dp', 'sc', 'core'))  418 us
    reduce_scatter x4, waiting for transfers between devices, on_device(): lax.psum_scatter(value_term.astype(jnp.bfloat16).reshape(seq_total, group...  173 us
    all_gather x4, waiting for transfers between devices, on_device(): v_all = lax.all_gather(chip_v[:, cols], 'sc', axis=0, tiled=True)  158 us
    all_gather x4, waiting for transfers between devices, on_device(): k_all = lax.all_gather(chip_k[:, cols], 'sc', axis=0, tiled=True)  58.5 us
    reduce_scatter x4, waiting for transfers between devices, on_device(): lax.psum_scatter(key_term.astype(jnp.bfloat16).reshape(seq_total, group_w...  57.8 us
    dot_general x4, matrix products, on_device(): jnp.einsum('htu,thd->uhd', dscore, q_part, preferred_element_type=jnp.flo...  38.7 us
    ppermute x2, waiting for transfers between devices, padded(): after = lax.ppermute(value[:width], SEQ, down)  33.3 us
    dot_general x4, matrix products, on_device(): jnp.einsum('htu,uhd->thd', dscore, k_part, preferred_element_type=jnp.flo...  32.6 us
  transfers between devices with their start and end apart: 22, of which 18 were waited for; matrix products, arithmetic and copies ran while one was open for 16% of the time, Pallas kernels for 0%

profile of v1, /device:TPU:1, one launch (start us, length us, event | category | flops | bytes accessed | tf_op | source)
XLA Modules:
  0.0 1167.2 jit_solution(9703639769028915790)
XLA Ops:
  8.6 7.2 all_to_all.120
  36.2 21.2 %collective-permute-done.2 = bf16[3,2048]{0,1:T(8,128)(2,1)S(1)} collective-permute-done((bf16[3,2048]{0,1:T(8,128)(2,1)}, bf16[3,2048]{0,1:T(8,128)(2,1)S(1)}, u32[]{:S(2)}, u32[]{:S(2)}) %collective-permute-start.2) | collective-permute-done | bytes 12320 | tf_op jit(solution)/shard_map/ppermute | solution.py:21
  58.1 5.9 fusion.115
  71.0 33.9 %all-gather.18.cloned.1.call-done = bf16[2048,256]{1,0:T(8,128)(2,1)} async-done(((bf16[256,256]{1,0:T(8,128)(2,1)}), bf16[2048,256]{1,0:T(8,128)(2,1)}) %all-gather.18.cloned.1.call-update) | async-done | bytes 1048592 | tf_op jit(solution)/shard_map/all_gather | solution.py:74
  115.8 9.7 convolution_convert_fusion.2
  127.2 19.8 %all-gather.20.cloned.1.call-done = bf16[2048,256]{1,0:T(8,128)(2,1)} async-done(((bf16[256,256]{1,0:T(8,128)(2,1)}), bf16[2048,256]{1,0:T(8,128)(2,1)}) %all-gather.20.cloned.1.call-update) | async-done | bytes 1048592 | tf_op jit(solution)/shard_map/all_gather | solution.py:73
  149.3 41.2 %all-gather.22.cloned.1.call-done = bf16[2048,256]{1,0:T(8,128)(2,1)} async-done(((bf16[256,256]{1,0:T(8,128)(2,1)}), bf16[2048,256]{1,0:T(8,128)(2,1)}) %all-gather.22.cloned.1.call-update) | async-done | bytes 1048592 | tf_op jit(solution)/shard_map/all_gather | solution.py:74
  195.7 6.5 fusion.179
  202.2 9.7 convolution_convert_fusion.1
  213.7 19.4 %all-gather.24.cloned.1.call-done = bf16[2048,256]{1,0:T(8,128)(2,1)} async-done(((bf16[256,256]{1,0:T(8,128)(2,1)}), bf16[2048,256]{1,0:T(8,128)(2,1)}) %all-gather.24.cloned.1.call-update) | async-done | bytes 1048592 | tf_op jit(solution)/shard_map/all_gather | solution.py:73
  235.3 41.3 %all-gather.26.cloned.1.call-done = bf16[2048,256]{1,0:T(8,128)(2,1)} async-done(((bf16[256,256]{1,0:T(8,128)(2,1)}), bf16[2048,256]{1,0:T(8,128)(2,1)}) %all-gather.26.cloned.1.call-update) | async-done | bytes 1048592 | tf_op jit(solution)/shard_map/all_gather | solution.py:74
  282.8 6.6 fusion.178
  289.4 9.7 convolution_convert_fusion
  300.2 19.3 %all-gather.12.cloned.1.call-done = bf16[2048,256]{1,0:T(8,128)(2,1)} async-done(((bf16[256,256]{1,0:T(8,128)(2,1)}), bf16[2048,256]{1,0:T(8,128)(2,1)}) %all-gather.12.cloned.1.call-update) | async-done | bytes 1048592 | tf_op jit(solution)/shard_map/all_gather | solution.py:73
  321.7 41.5 %all-gather.14.cloned.1.call-done = bf16[2048,256]{1,0:T(8,128)(2,1)} async-done(((bf16[256,256]{1,0:T(8,128)(2,1)}), bf16[2048,256]{1,0:T(8,128)(2,1)}) %all-gather.14.cloned.1.call-update) | async-done | bytes 1048592 | tf_op jit(solution)/shard_map/all_gather | solution.py:74
  369.5 6.3 fusion.181
  375.8 9.7 convolution_convert_fusion.3
  414.1 9.1 all_to_all.123
  425.9 12.1 %collective-permute-done.1 = bf16[3,2048]{0,1:T(8,128)(2,1)S(1)} collective-permute-done((bf16[3,2048]{0,1:T(8,128)(2,1)S(1)}, bf16[3,2048]{0,1:T(8,128)(2,1)S(1)}, u32[]{:S(2)}, u32[]{:S(2)}) %collective-permute-start.1) | collective-permute-done | bytes 12320 | tf_op jit(solution)/shard_map/ppermute | solution.py:21
  442.1 8.2 fusion.91
  450.6 8.2 fusion.94
  459.0 8.1 fusion.97
  467.4 8.1 fusion.88
  485.9 14.4 %reduce-scatter.15.cloned.1.call-done = bf16[256,256]{0,1:T(8,128)(2,1)} async-done(((bf16[2048,256]{0,1:T(8,128)(2,1)}), bf16[256,256]{0,1:T(8,128)(2,1)}) %reduce-scatter.15.cloned.1.call-update) | async-done | bytes 131088 | tf_op jit(solution)/shard_map/reduce_scatter | solution.py:100
  500.3 43.4 %reduce-scatter.9.cloned.1.call-done = bf16[256,256]{0,1:T(8,128)(2,1)} async-done(((bf16[2048,256]{0,1:T(8,128)(2,1)}), bf16[256,256]{0,1:T(8,128)(2,1)}) %reduce-scatter.9.cloned.1.call-update) | async-done | bytes 131088 | tf_op jit(solution)/shard_map/reduce_scatter | solution.py:100
  545.0 42.2 %reduce-scatter.19.cloned.1.call-done = bf16[256,256]{0,1:T(8,128)(2,1)} async-done(((bf16[2048,256]{0,1:T(8,128)(2,1)}), bf16[256,256]{0,1:T(8,128)(2,1)}) %reduce-scatter.19.cloned.1.call-update) | async-done | bytes 131088 | tf_op jit(solution)/shard_map/reduce_scatter | solution.py:108
  587.3 43.4 %reduce-scatter.21.cloned.1.call-done = bf16[256,256]{0,1:T(8,128)(2,1)} async-done(((bf16[2048,256]{0,1:T(8,128)(2,1)}), bf16[256,256]{0,1:T(8,128)(2,1)}) %reduce-scatter.21.cloned.1.call-update) | async-done | bytes 131088 | tf_op jit(solution)/shard_map/reduce_scatter | solution.py:108
  630.6 43.4 %reduce-scatter.23.cloned.1.call-done = bf16[256,256]{0,1:T(8,128)(2,1)} async-done(((bf16[2048,256]{0,1:T(8,128)(2,1)}), bf16[256,256]{0,1:T(8,128)(2,1)}) %reduce-scatter.23.cloned.1.call-update) | async-done | bytes 131088 | tf_op jit(solution)/shard_map/reduce_scatter | solution.py:108
  674.0 43.5 %reduce-scatter.17.cloned.1.call-done = bf16[256,256]{0,1:T(8,128)(2,1)} async-done(((bf16[2048,256]{0,1:T(8,128)(2,1)}), bf16[256,256]{0,1:T(8,128)(2,1)}) %reduce-scatter.17.cloned.1.call-update) | async-done | bytes 131088 | tf_op jit(solution)/shard_map/reduce_scatter | solution.py:108
  718.9 9.2 all_to_all.125
  734.8 418.1 %all-gather.28.cloned.1.call-done = f32[256,7,2048]{2,1,0:T(8,128)} async-done(((f32[1,7,2048]{2,1,0:T(8,128)}), f32[256,7,2048]{2,1,0:T(8,128)}) %all-gather.28.cloned.1.call-update) | async-done | bytes 14680080 | tf_op jit(solution)/shard_map/all_gather | solution.py:128
  1152.9 7.6 reduce_sum.159
  (174 shorter events, 124.6 us)
Async XLA Ops:
  7.2 9.7 copy-start.3
  7.2 62.3 %all-gather.16.cloned.1.call-start = ((), (), s32[]{:S(2)}) async-start(), calls=%async_computation.18 | async-start | bytes 1179648 | tf_op jit(solution)/shard_map/all_gather | solution.py:73
  8.6 17.0 %copy-start.4 = (bf16[1,128,2048]{2,1,0:T(8,128)(2,1)S(1)}, bf16[1,128,2048]{2,1,0:T(8,128)(2,1)}, u32[]{:S(2)}) copy-start(bf16[1,128,2048]{2,1,0:T(8,128)(2,1)} %param.5) | copy-start | bytes 1572868
  16.0 14.5 %copy-start.5 = (bf16[1,128,2048]{2,1,0:T(8,128)(2,1)S(1)}, bf16[1,128,2048]{2,1,0:T(8,128)(2,1)}, u32[]{:S(2)}) copy-start(bf16[1,128,2048]{2,1,0:T(8,128)(2,1)} %param.8) | copy-start | bytes 1572868
  16.8 88.0 %all-gather.18.cloned.1.call-start = ((), (), s32[]{:S(2)}) async-start(), calls=%async_computation.19 | async-start | bytes 1179648 | tf_op jit(solution)/shard_map/all_gather | solution.py:74
  21.3 12.2 %copy-start.16 = (f32[7,2048]{1,0:T(8,128)S(1)}, f32[7,2048]{1,0:T(8,128)}, u32[]{:S(2)}) copy-start(f32[7,2048]{1,0:T(8,128)} %param.9) | copy-start | bytes 172036
  22.4 124.7 %all-gather.20.cloned.1.call-start = ((), (), s32[]{:S(2)}) async-start(), calls=%async_computation.20 | async-start | bytes 1179648 | tf_op jit(solution)/shard_map/all_gather | solution.py:73
  23.1 167.5 %all-gather.22.cloned.1.call-start = ((), (), s32[]{:S(2)}) async-start(), calls=%async_computation.21 | async-start | bytes 1179648 | tf_op jit(solution)/shard_map/all_gather | solution.py:74
  23.7 209.4 %all-gather.24.cloned.1.call-start = ((), (), s32[]{:S(2)}) async-start(), calls=%async_computation.22 | async-start | bytes 1179648 | tf_op jit(solution)/shard_map/all_gather | solution.py:73
  24.3 252.4 %all-gather.26.cloned.1.call-start = ((), (), s32[]{:S(2)}) async-start(), calls=%async_computation.23 | async-start | bytes 1179648 | tf_op jit(solution)/shard_map/all_gather | solution.py:74
  24.8 294.7 %all-gather.12.cloned.1.call-start = ((), (), s32[]{:S(2)}) async-start(), calls=%async_computation.16 | async-start | bytes 1179648 | tf_op jit(solution)/shard_map/all_gather | solution.py:73
  26.6 8.0 all-to-all-start
  30.4 332.8 %all-gather.14.cloned.1.call-start = ((), (), s32[]{:S(2)}) async-start(), calls=%async_computation.17 | async-start | bytes 1179648 | tf_op jit(solution)/shard_map/all_gather | solution.py:74
  31.7 25.8 %collective-permute-start.2 = (bf16[3,2048]{0,1:T(8,128)(2,1)}, bf16[3,2048]{0,1:T(8,128)(2,1)S(1)}, u32[]{:S(2)}, u32[]{:S(2)}) collective-permute-start(bf16[3,2048]{0,1:T(8,128)(2,1)} %get-tuple-element.38), channel_id=1, source_target_pairs={{1,0},{2,1},{3,2},{4,3},{5,4},{6,5},{7,6},{8,7},{9,8},{10,9},{11,1... | collective-permute-start | bytes 36872 | tf_op jit(solution)/shard_map/ppermute | solution.py:21
  31.8 26.3 %collective-permute-start.3 = (bf16[3,2048]{0,1:T(8,128)(2,1)S(1)}, bf16[3,2048]{0,1:T(8,128)(2,1)}, u32[]{:S(2)}, u32[]{:S(2)}) collective-permute-start(bf16[3,2048]{0,1:T(8,128)(2,1)S(1)} %get-tuple-element.39), channel_id=1, source_target_pairs={{0,1},{1,2},{2,3},{3,4},{4,5},{5,6},{6,7},{7,8},{8,9},{9,10},{10,1... | collective-permute-start | bytes 36872 | tf_op jit(solution)/shard_map/ppermute | solution.py:20
  33.5 452.4 %reduce-scatter.11.cloned.1.call-start = ((), (), s32[]{:S(2)}) async-start(), calls=%async_computation.25 | async-start | bytes 1179648 | tf_op jit(solution)/shard_map/reduce_scatter | solution.py:100
  71.0 44.8 %copy-start.2 = (bf16[2048,256]{0,1:T(8,128)(2,1)}, bf16[2048,256]{0,1:T(8,128)(2,1)S(1)}, u32[]{:S(2)}) copy-start(bf16[2048,256]{0,1:T(8,128)(2,1)S(1)} %copy.289) | copy-start | bytes 3145732
  115.8 9.9 copy-start.6
  115.8 10.7 copy-start.7
  125.5 360.4 %reduce-scatter.13.cloned.1.call-start = ((), (), s32[]{:S(2)}) async-start(), calls=%async_computation.26 | async-start | bytes 1179648 | tf_op jit(solution)/shard_map/reduce_scatter | solution.py:100
  211.9 288.5 %reduce-scatter.15.cloned.1.call-start = ((), (), s32[]{:S(2)}) async-start(), calls=%async_computation.27 | async-start | bytes 1179648 | tf_op jit(solution)/shard_map/reduce_scatter | solution.py:100
  299.1 244.6 %reduce-scatter.9.cloned.1.call-start = ((), (), s32[]{:S(2)}) async-start(), calls=%async_computation.24 | async-start | bytes 1179648 | tf_op jit(solution)/shard_map/reduce_scatter | solution.py:100
  321.7 47.7 %copy-start.10 = (bf16[256,256]{0,1:T(8,128)(2,1)S(1)}, bf16[256,256]{0,1:T(8,128)(2,1)}, u32[]{:S(2)}) copy-start(bf16[256,256]{0,1:T(8,128)(2,1)} %copy.277) | copy-start | bytes 393220
  375.8 9.8 copy-start.8
  375.8 9.8 copy-start.17
  385.6 201.7 %reduce-scatter.19.cloned.1.call-start = ((), (), s32[]{:S(2)}) async-start(), calls=%async_computation.29 | async-start | bytes 1179648 | tf_op jit(solution)/shard_map/reduce_scatter | solution.py:108
  389.4 241.2 %reduce-scatter.21.cloned.1.call-start = ((), (), s32[]{:S(2)}) async-start(), calls=%async_computation.30 | async-start | bytes 1179648 | tf_op jit(solution)/shard_map/reduce_scatter | solution.py:108
  393.3 280.8 %reduce-scatter.23.cloned.1.call-start = ((), (), s32[]{:S(2)}) async-start(), calls=%async_computation.31 | async-start | bytes 1179648 | tf_op jit(solution)/shard_map/reduce_scatter | solution.py:108
  397.1 320.4 %reduce-scatter.17.cloned.1.call-start = ((), (), s32[]{:S(2)}) async-start(), calls=%async_computation.28 | async-start | bytes 1179648 | tf_op jit(solution)/shard_map/reduce_scatter | solution.py:108
  407.5 745.4 %all-gather.28.cloned.1.call-start = ((), (), s32[]{:S(2)}) async-start(), calls=%async_computation.32 | async-start | bytes 16842752 | tf_op jit(solution)/shard_map/all_gather | solution.py:128
  423.9 1.6 collective-permute-start
  424.4 13.6 %collective-permute-start.1 = (bf16[3,2048]{0,1:T(8,128)(2,1)S(1)}, bf16[3,2048]{0,1:T(8,128)(2,1)S(1)}, u32[]{:S(2)}, u32[]{:S(2)}) collective-permute-start(bf16[3,2048]{0,1:T(8,128)(2,1)S(1)} %bitcast.223), channel_id=1, source_target_pairs={{1,0},{2,1},{3,2},{4,3},{5,4},{6,5},{7,6},{8,7},{9,8},{10,9},{11,1... | collective-permute-start | bytes 36872 | tf_op jit(solution)/shard_map/ppermute | solution.py:21
  (11 other events, 50.2 us)
Sparse Core Ops, SparseCore 0:
  17.0 45.7 all-gather.15
  64.5 40.3 all-gather.17
  106.7 40.3 all-gather.19
  148.7 41.8 all-gather.21
  192.2 40.8 all-gather.23
  235.3 41.2 all-gather.25
  278.4 41.0 all-gather.11
  321.9 41.3 all-gather.13
  365.8 41.8 reduce-scatter.10
  410.0 47.2 reduce-scatter.12
  459.9 40.3 reduce-scatter.14
  502.7 40.9 reduce-scatter.8
  546.2 40.9 reduce-scatter.18
  589.6 40.9 reduce-scatter.20
  633.0 40.9 reduce-scatter.22
  676.4 41.0 reduce-scatter.16
  719.9 433.0 all-gather.27
